TPU v7x, 32 devices: a whole 2x2x4 slice. The times are simulated.
32 devices in a mesh: narrow: 8 (over z, x), wide: 4 (over y, core).
Axes of the slice: x: 2, y: 2, z: 4, core: 2. Of those that a mesh axis runs over, the one named last changes fastest.
Arguments:
- amps: bfloat16 [16, 512, 512], P(None, 'narrow', 'wide'), may hold values from -1 to 1
- left_fit: bfloat16 [64, 512, 256], P(None, 'narrow'), may hold values from -0.375 to 0.375
- right_fit: bfloat16 [512, 512, 256], P('narrow', 'wide'), may hold values from -0.375 to 0.375
- pair_list: int32 [16, 2], P('narrow'), may hold values from 0 to 127, as said below
- occ_energy: float32 [128], replicated, may hold values from -2 to -0.5
- vir_energy: float32 [512], replicated, may hold values from 0.5 to 3
Outputs:
- update: float32 [16, 64, 512], P('narrow', None, 'wide')
Inputs may be any that keep to these rules, and one draw needn't show every extreme that they name: `pair_list`: each row (i, j) has i <= j.
All inputs are finite; a program needn't handle non-finite values.
Results may differ from a plain program's by a relative error of at most 0.0029.
Values may be sent and summed in bfloat16 or wider, within the bound.
No kernel may reach another device: no remote copies, remote signals or barrier semaphores. Data moves between devices by JAX's collectives and lax.ppermute only.
A program may use at most 128 MiB of HBM per device.

v0:
```python
import jax
import jax.numpy as jnp
from jax import lax
from jax.sharding import PartitionSpec as P

GROUPS = 2


def make_body(n_narrow, n_wide):
    span = n_narrow // GROUPS

    def body(amps, left_fit, right_fit, pair_list, occ_energy, vir_energy):
        n = lax.axis_index("narrow")
        w = lax.axis_index("wide")
        r = n % span
        g = n // span
        b_blk, d_blk, aux = right_fit.shape
        q_blk = aux // span
        rows, c_blk, _ = left_fit.shape
        pairs = amps.shape[0]
        vir_total = b_blk * n_narrow
        amps_all = lax.all_gather(amps, "narrow", axis=1, tiled=True)
        c_sub = c_blk // n_wide
        left_part = lax.dynamic_slice_in_dim(left_fit, w * c_sub, c_sub, 1)
        left_part = left_part.reshape(rows, c_sub, span, q_blk).transpose(2, 0, 1, 3)
        left_send = jnp.concatenate([left_part] * GROUPS, axis=0)
        left_recv = lax.all_to_all(left_send, "narrow", 0, 0, tiled=True)
        left_all = lax.all_gather(left_recv, "wide", axis=0, tiled=False)
        left_all = left_all.transpose(2, 1, 0, 3, 4).reshape(rows, c_blk * n_narrow, q_blk)
        right_split = right_fit.reshape(b_blk, d_blk, span, q_blk)
        chunks = []
        for shift in range(span):
            dest = (r + shift) % span
            piece = lax.dynamic_index_in_dim(right_split, dest, 2, keepdims=False)
            if shift:
                perm = [
                    (gg * span + i, gg * span + (i + shift) % span)
                    for gg in range(GROUPS)
                    for i in range(span)
                ]
                piece = lax.ppermute(piece, "narrow", perm)
            chunks.append(piece)
        inter = jnp.einsum(
            "acq,pcd->padq", left_all, amps_all, preferred_element_type=jnp.float32
        ).astype(jnp.bfloat16)
        right_group = jnp.concatenate(chunks, axis=0)
        part = lax.dot_general(
            inter.reshape(pairs * rows, d_blk * q_blk),
            right_group.reshape(span * b_blk, d_blk * q_blk),
            (((1,), (1,)), ((), ())),
            preferred_element_type=jnp.float32,
        ).reshape(pairs, rows, span, b_blk)
        flipped = jnp.concatenate(
            [part[:, :, (span - k) % span : (span - k) % span + 1] for k in range(span)] * 2, axis=2
        )
        ordered = lax.dynamic_slice_in_dim(flipped, span - r, span, 2)
        ordered = ordered.reshape(pairs, rows, span * b_blk)
        pad = jnp.zeros((pairs, rows, (GROUPS - 1) * span * b_blk), jnp.float32)
        padded = jnp.concatenate([pad, ordered, pad], axis=2)
        ladder = lax.dynamic_slice_in_dim(padded, (GROUPS - 1 - g) * span * b_blk, vir_total, 2)
        ladder = lax.psum_scatter(ladder, "wide", scatter_dimension=2, tiled=True)
        ladder = lax.psum_scatter(ladder, "narrow", scatter_dimension=0, tiled=True)
        local_cols = ladder.shape[2]
        occ_ids = jnp.arange(occ_energy.shape[0], dtype=jnp.int32)
        occ_first = jnp.sum(
            jnp.where(pair_list[:, 0:1] == occ_ids[None, :], occ_energy[None, :], 0.0), axis=1
        )
        occ_second = jnp.sum(
            jnp.where(pair_list[:, 1:2] == occ_ids[None, :], occ_energy[None, :], 0.0), axis=1
        )
        vir_cols = lax.dynamic_slice_in_dim(vir_energy, w * local_cols, local_cols, 0)
        vir_rows = vir_energy[:rows]
        denominator = (
            (occ_first + occ_second)[:, None, None]
            - vir_rows[None, :, None]
            - vir_cols[None, None, :]
        )
        return ladder / denominator

    return body


def solution(mesh):
    return jax.shard_map(
        make_body(mesh.shape["narrow"], mesh.shape["wide"]),
        mesh=mesh,
        in_specs=(
            P(None, "narrow", "wide"),
            P(None, "narrow", None),
            P("narrow", "wide", None),
            P("narrow", None),
            P(),
            P(),
        ),
        out_specs=P("narrow", None, "wide"),
        check_vma=False,
    )
```

profile of v0, /device:TPU:0, one launch (start us, length us, event | category | flops | bytes accessed | tf_op | source)
XLA Modules:
  0.0 375.9 jit_solution(8755748005040324394)
XLA Ops:
  6.5 1.6 copy-done
  9.0 2.0 reshape.61
  12.2 1.7 copy.46
  13.9 3.4 reshape.73
  17.3 32.8 %all_to_all.5 = bf16[8,2,32768]{2,1,0:T(2,128)(2,1)S(1)} all-to-all(bf16[8,2,32768]{2,1,0:T(2,128)(2,1)S(1)} %reshape.73), channel_id=1, replica_groups=mesh['narrow'=8,'wide'=4] {'narrow'}, dimensions={0} | all-to-all | bytes 2097152 | tf_op jit(solution)/shard_map/all_to_all | solution.py:27
  50.1 2.7 reshape.74
  53.7 6.4 %copy.50 = bf16[64,128,256]{1,2,0:T(8,128)(2,1)} copy(bf16[64,128,256]{2,1,0:T(8,128)(2,1)} %param.8) | data formatting | bytes 8388608 | tf_op args[2]
  60.1 5.1 %constant_dynamic-slice_fusion.1 = (bf16[64,128,1,64]{1,3,2,0:T(8,128)(2,1)S(1)}, bf16[64,128,64]{1,2,0:T(8,128)(2,1)}, bf16[64,128,64]{1,2,0:T(8,128)(2,1)}, bf16[64,128,64]{1,2,0:T(8,128)(2,1)}) fusion(bf16[64,128,4,64]{1,3,2,0:T(8,128)(2,1)} %bitcast.36, s32[]{:T(128)S(6)} %select_n.62, s32[]{:T(128)S(6)} %select_n.68, s32[]{:T(128)S(6)} %select_n.66, ...), kind=kLoop, calls=%fused_computation.24 | loop fusion | bytes 8388624 | tf_op jit(solution)/shard_map/jit(dynamic_index_in_dim)/dynamic_slice | solution.py:34
  65.2 1.6 collective-permute-start
  66.8 2.6 collective-permute-start.2
  70.5 1.7 concatenate.22
  72.2 20.3 %collective-permute-done = bf16[64,128,64]{1,2,0:T(8,128)(2,1)} collective-permute-done((bf16[64,128,64]{1,2,0:T(8,128)(2,1)}, bf16[64,128,64]{1,2,0:T(8,128)(2,1)}, u32[]{:S(2)}, u32[]{:S(2)}) %collective-permute-start) | collective-permute-done | bytes 1048608 | tf_op jit(solution)/shard_map/ppermute | solution.py:41
  92.5 2.0 copy.52
  94.6 2.5 concatenate.23
  97.0 2.0 copy.53
  99.1 2.5 concatenate.24
  101.6 11.2 %collective-permute-done.2 = bf16[64,128,64]{1,2,0:T(8,128)(2,1)} collective-permute-done((bf16[64,128,64]{1,2,0:T(8,128)(2,1)}, bf16[64,128,64]{1,2,0:T(8,128)(2,1)}, u32[]{:S(2)}, u32[]{:S(2)}) %collective-permute-start.2) | collective-permute-done | bytes 1048608 | tf_op jit(solution)/shard_map/ppermute | solution.py:41
  112.7 2.0 copy.54
  114.8 2.5 concatenate.25
  117.3 3.6 pad_maximum_fusion
  120.9 9.1 %copy.47 = bf16[64,8,4,16,64]{4,3,2,1,0:T(8,128)(2,1)} copy(bf16[64,8,4,16,64]{4,3,0,1,2:T(8,128)(2,1)} %bitcast.37) | data formatting | bytes 8388608 | tf_op jit(solution)/shard_map/transpose | solution.py:29
  130.1 31.7 %all-gather.4.cloned.1.call-done = bf16[16,512,128]{2,1,0:T(8,128)(2,1)} async-done(((bf16[16,64,128]{2,1,0:T(8,128)(2,1)}), bf16[16,512,128]{2,1,0:T(8,128)(2,1)}) %all-gather.4.cloned.1.call-update) | async-done | bytes 2097168 | tf_op jit(solution)/shard_map/all_gather | solution.py:22
  161.8 16.0 %convert_bitcast_fusion = bf16[16,64,128,64]{2,3,0,1:T(8,128)(2,1)} fusion(bf16[64,512,64,1]{2,1,3,0:T(8,128)(2,1)} %bitcast.35, bf16[16,512,128]{2,1,0:T(8,128)(2,1)} %all-gather.4.cloned.1.call-done), kind=kOutput, calls=%fused_computation.2 | convolution fusion | flops 8598323200 | bytes 23068672 | tf_op jit(solution)/shard_map/acq,pcd->padq/dot_general | solution.py:43
  177.8 30.3 %copy.49 = bf16[16,64,128,64]{3,2,1,0:T(8,128)(2,1)} copy(bf16[16,64,128,64]{2,3,0,1:T(8,128)(2,1)} %convert_bitcast_fusion) | data formatting | bytes 33554432 | tf_op jit(solution)/shard_map/convert_element_type | solution.py:45
  208.1 44.0 %reshape.68 = bf16[16,64,8192,1]{2,1,0,3:T(8,128)(2,1)} reshape(bf16[16,64,128,64]{3,2,1,0:T(8,128)(2,1)} %copy.49) | data formatting | bytes 33554432 | tf_op jit(solution)/shard_map/dot_general | solution.py:47
  252.1 12.2 %fusion = f32[16,64,4,64]{3,1,2,0:T(8,128)S(1)} fusion(bf16[4,64,8192,1]{2,1,0,3:T(8,128)(2,1)} %bitcast.39, bf16[16,64,8192,1]{2,1,0,3:T(8,128)(2,1)} %reshape.68), kind=kOutput, calls=%fused_computation | convolution fusion | flops 4294967296 | bytes 22020096 | tf_op jit(solution)/shard_map/dot_general | solution.py:47
  264.8 2.8 copy.55
  267.6 2.6 reshape.64
  270.4 1.7 fusion.3
  272.2 30.0 %reduce-scatter.3.cloned.1.call-done = f32[16,64,128]{2,1,0:T(8,128)} async-done(((f32[16,64,512]{2,1,0:T(8,128)}), f32[16,64,128]{2,1,0:T(8,128)}) %reduce-scatter.3.cloned.1.call-update) | async-done | bytes 524304 | tf_op jit(solution)/shard_map/reduce_scatter | solution.py:61
  302.8 64.9 %reduce-scatter.5.cloned.1.call-done = f32[2,64,128]{2,1,0:T(8,128)} async-done(((f32[16,64,128]{2,1,0:T(8,128)}), f32[2,64,128]{2,1,0:T(8,128)}) %reduce-scatter.5.cloned.1.call-update) | async-done | bytes 65552 | tf_op jit(solution)/shard_map/reduce_scatter | solution.py:62
  367.8 1.6 subtract_divide_fusion
  (40 shorter events, 5.1 us)
Async XLA Ops:
  6.5 1.6 copy-start
  6.5 114.4 %all-gather.6.cloned.1.call-start = ((), (), s32[]{:S(2)}) async-start(), calls=%async_computation.6 | async-start | bytes 10485760 | tf_op jit(solution)/shard_map/all_gather | solution.py:28
  52.8 109.0 %all-gather.4.cloned.1.call-start = ((), (), s32[]{:S(2)}) async-start(), calls=%async_computation.3 | async-start | bytes 2359296 | tf_op jit(solution)/shard_map/all_gather | solution.py:22
  53.5 248.7 %reduce-scatter.3.cloned.1.call-start = ((), (), s32[]{:S(2)}) async-start(), calls=%async_computation.4 | async-start | bytes 2621440 | tf_op jit(solution)/shard_map/reduce_scatter | solution.py:61
  65.2 27.3 %collective-permute-start = (bf16[64,128,64]{1,2,0:T(8,128)(2,1)}, bf16[64,128,64]{1,2,0:T(8,128)(2,1)}, u32[]{:S(2)}, u32[]{:S(2)}) collective-permute-start(bf16[64,128,64]{1,2,0:T(8,128)(2,1)} %get-tuple-element.12), channel_id=1, source_target_pairs={{0,4},{4,8},{8,12},{12,0},{16,20},{20,24},{24,28},{28,16},{1,5},{5... | collective-permute-start | bytes 3145736 | tf_op jit(solution)/shard_map/ppermute | solution.py:41
  66.8 30.2 %collective-permute-start.1 = (bf16[64,128,64]{1,2,0:T(8,128)(2,1)}, bf16[64,128,64]{1,2,0:T(8,128)(2,1)}, u32[]{:S(2)}, u32[]{:S(2)}) collective-permute-start(bf16[64,128,64]{1,2,0:T(8,128)(2,1)} %get-tuple-element.11), channel_id=1, source_target_pairs={{0,8},{4,12},{8,0},{12,4},{16,24},{20,28},{24,16},{28,20},{1,9},{5... | collective-permute-start | bytes 3145736 | tf_op jit(solution)/shard_map/ppermute | solution.py:41
  66.8 45.9 %collective-permute-start.2 = (bf16[64,128,64]{1,2,0:T(8,128)(2,1)}, bf16[64,128,64]{1,2,0:T(8,128)(2,1)}, u32[]{:S(2)}, u32[]{:S(2)}) collective-permute-start(bf16[64,128,64]{1,2,0:T(8,128)(2,1)} %get-tuple-element.10), channel_id=1, source_target_pairs={{0,12},{4,0},{8,4},{12,8},{16,28},{20,16},{24,20},{28,24},{1,13},{... | collective-permute-start | bytes 3145736 | tf_op jit(solution)/shard_map/ppermute | solution.py:41
  267.6 101.7 %copy-start.1 = (bf16[64,64,256]{2,1,0:T(8,128)(2,1)S(1)}, bf16[64,64,256]{2,1,0:T(8,128)(2,1)}, u32[]{:S(2)}) copy-start(bf16[64,64,256]{2,1,0:T(8,128)(2,1)} %param.7) | copy-start | bytes 6291460
  270.2 32.0 %copy-start.4 = (f32[512]{0:T(512)S(1)}, f32[512]{0:T(512)}, u32[]{:S(2)}) copy-start(f32[512]{0:T(512)} %param.11) | copy-start | bytes 6148
  270.2 32.1 %copy-start.2 = (s32[2,2]{1,0:T(2,128)S(1)}, s32[2,2]{1,0:T(2,128)}, u32[]{:S(2)}) copy-start(s32[2,2]{1,0:T(2,128)} %param.9) | copy-start | bytes 52
  270.2 32.3 %copy-start.3 = (f32[128]{0:T(128)S(1)}, f32[128]{0:T(128)}, u32[]{:S(2)}) copy-start(f32[128]{0:T(128)} %param.10) | copy-start | bytes 1540
  270.2 32.5 %slice-start = ((f32[512]{0:T(512)}), f32[64]{0:T(128)S(1)}, s32[]{:S(2)}) async-start(f32[512]{0:T(512)} %param.11), calls=%async_computation.7 | async-start | bytes 1024 | tf_op jit(solution)/shard_map/slice | solution.py:72
  272.1 95.6 %reduce-scatter.5.cloned.1.call-start = ((), (), s32[]{:S(2)}) async-start(), calls=%async_computation.5 | async-start | bytes 589824 | tf_op jit(solution)/shard_map/reduce_scatter | solution.py:62
Sparse Core Ops, SparseCore 0:
  52.9 57.3 all-gather.5
  112.4 49.2 all-gather.3
  272.2 29.9 reduce-scatter.2
  305.8 61.9 reduce-scatter.4
where the time goes:
time: 378 us; the launch traced here: 376 us
  waiting for transfers between devices  159 us (42%)
  local copies, waits for them, and re-layouts  130 us (34%)
  blocking collectives  32.8 us (9%)
  matrix products  28.2 us (7%)
  between operations  13.5 us (4%)
  other arithmetic  8.46 us (2%)
  starting transfers between devices  4.34 us (1%)
    reduce_scatter x1, waiting for transfers between devices, body(): ladder = lax.psum_scatter(ladder, 'narrow', scatter_dimension=0, tiled=True)  64.9 us
    dot_general x1, local copies, waits for them, and re-layouts, body(): lax.dot_general(inter.reshape(pairs * rows, d_blk * q_blk), right_group.r...  44 us
    all_to_all x1, blocking collectives, body(): left_recv = lax.all_to_all(left_send, 'narrow', 0, 0, tiled=True)  32.8 us
    all_gather x1, waiting for transfers between devices, body(): amps_all = lax.all_gather(amps, 'narrow', axis=1, tiled=True)  31.7 us
    ppermute x3, waiting for transfers between devices, body(): piece = lax.ppermute(piece, 'narrow', perm)  31.5 us
    convert_element_type x1, local copies, waits for them, and re-layouts, body(): inter = jnp.einsum('acq,pcd->padq', left_all, amps_all, preferred_element...  30.3 us
    reduce_scatter x1, waiting for transfers between devices, body(): ladder = lax.psum_scatter(ladder, 'wide', scatter_dimension=2, tiled=True)  30 us
    dot_general x1, matrix products, body(): jnp.einsum('acq,pcd->padq', left_all, amps_all, preferred_element_type=jn...  16 us
  transfers between devices with their start and end apart: 7, of which 5 were waited for; matrix products, arithmetic and copies ran while one was open for 11% of the time, Pallas kernels for 0%

commit v1 on v0

--- a/solution.py
+++ b/solution.py
@@ -4,6 +4,18 @@
 from jax.sharding import PartitionSpec as P
 
 GROUPS = 2
+
+
+def in_blocks(x, dim, size):
+    shape = x.shape
+    tiles = x.reshape(*shape[:dim], size, shape[dim] // size, *shape[dim + 1 :])
+    return jnp.moveaxis(tiles, dim, 0)
+
+
+def joined_along(parts, dim):
+    parts = jnp.moveaxis(parts, 0, dim)
+    lengths = parts.shape
+    return parts.reshape(*lengths[:dim], lengths[dim] * lengths[dim + 1], *lengths[dim + 2 :])
 
 
 def make_body(n_narrow, n_wide):
@@ -24,7 +36,14 @@
         left_part = lax.dynamic_slice_in_dim(left_fit, w * c_sub, c_sub, 1)
         left_part = left_part.reshape(rows, c_sub, span, q_blk).transpose(2, 0, 1, 3)
         left_send = jnp.concatenate([left_part] * GROUPS, axis=0)
-        left_recv = lax.all_to_all(left_send, "narrow", 0, 0, tiled=True)
+        length, index = (lax.axis_size("narrow"), lax.axis_index("narrow"))
+        blocks = in_blocks(left_send, 0, length)
+        done = [blocks[index]]
+        for step in range(1, length):
+            sent = blocks[index ^ step]
+            done.append(lax.ppermute(sent, "narrow", [(i_2, i_2 ^ step) for i_2 in range(length)]))
+        blocks = jnp.stack(done)[index ^ jnp.arange(length)]
+        left_recv = joined_along(blocks, 0)
         left_all = lax.all_gather(left_recv, "wide", axis=0, tiled=False)
         left_all = left_all.transpose(2, 1, 0, 3, 4).reshape(rows, c_blk * n_narrow, q_blk)
         right_split = right_fit.reshape(b_blk, d_blk, span, q_blk)

time: 378 us -> 463 us (1.22)
  waiting for transfers between devices: 159 us -> 223 us
  starting transfers between devices: 4.34 us -> 38.7 us
  blocking collectives: 32.8 us -> 0 us
  other arithmetic: 8.46 us -> 35.4 us
  local copies, waits for them, and re-layouts: 130 us -> 123 us
    ppermute x0 -> x7, waiting for transfers between devices: none -> 62.7 us  [body(): lax.ppermute(sent, 'narrow', [(i_2, i_2 ^ step) for i_2 in range(length)])]
    all_to_all x1 -> x0, blocking collectives: 32.8 us -> none  [body(): left_recv = lax.all_to_all(left_send, 'narrow', 0, 0, tiled=True)]
    concatenate x1 -> x2, other arithmetic: 1.22 us -> 28.2 us  [body(): left_send = jnp.concatenate([left_part] * GROUPS, axis=0)]
    ppermute x3, starting transfers between devices: 4.21 us -> 24.5 us  [body(): piece = lax.ppermute(piece, 'narrow', perm)]
    ppermute x0 -> x7, starting transfers between devices: none -> 14 us  [body(): lax.ppermute(sent, 'narrow', [(i_2, i_2 ^ step) for i_2 in range(length)])]
    unnamed x20 -> x25, local copies, waits for them, and re-layouts: 14.3 us -> 9.66 us
  transfers between devices with their start and end apart: 7 -> 14, of which waited for: 5 -> 9; matrix products, arithmetic and copies ran while one was open for 11% -> 10% of each run, Pallas kernels for 0% -> 0%
where the time goes in v1:
time: 463 us; the launch traced here: 461 us
  waiting for transfers between devices  223 us (48%)
  local copies, waits for them, and re-layouts  123 us (27%)
  starting transfers between devices  38.7 us (8%)
  other arithmetic  35.4 us (8%)
  matrix products  28.3 us (6%)
  between operations  13.6 us (3%)
    reduce_scatter x1, waiting for transfers between devices, body(): ladder = lax.psum_scatter(ladder, 'narrow', scatter_dimension=0, tiled=True)  64.9 us
    ppermute x7, waiting for transfers between devices, body(): lax.ppermute(sent, 'narrow', [(i_2, i_2 ^ step) for i_2 in range(length)])  62.7 us
    dot_general x1, local copies, waits for them, and re-layouts, body(): lax.dot_general(inter.reshape(pairs * rows, d_blk * q_blk), right_group.r...  44 us
    all_gather x1, waiting for transfers between devices, body(): amps_all = lax.all_gather(amps, 'narrow', axis=1, tiled=True)  35.1 us
    convert_element_type x1, local copies, waits for them, and re-layouts, body(): inter = jnp.einsum('acq,pcd->padq', left_all, amps_all, preferred_element...  30.3 us
    reduce_scatter x1, waiting for transfers between devices, body(): ladder = lax.psum_scatter(ladder, 'wide', scatter_dimension=2, tiled=True)  30 us
    ppermute x3, waiting for transfers between devices, body(): piece = lax.ppermute(piece, 'narrow', perm)  29 us
    concatenate x2, other arithmetic, body(): left_send = jnp.concatenate([left_part] * GROUPS, axis=0)  28.2 us
  transfers between devices with their start and end apart: 14, of which 9 were waited for; matrix products, arithmetic and copies ran while one was open for 10% of the time, Pallas kernels for 0%

profile of v1, /device:TPU:0, one launch (start us, length us, event | category | flops | bytes accessed | tf_op | source)
XLA Modules:
  0.0 461.1 jit_solution(15180232323310994005)
XLA Ops:
  8.6 23.3 %fusion.5 = (bf16[1,64,16,64]{3,0,2,1:T(2,128)(2,1)S(1)}, bf16[1,64,16,64]{3,0,2,1:T(2,128)(2,1)}, bf16[1,64,16,64]{3,0,2,1:T(2,128)(2,1)}, bf16[1,64,16,64]{3,0...) fusion(s32[]{:T(128)S(6)} %select_n.101, ...), kind=kLoop, calls=%fused_computation.30 | loop fusion | flops 1572864 | bytes 1310744 | tf_op jit(solution)/shard_map/concatenate | solution.py:38
  31.9 3.0 collective-permute-start.1
  34.9 4.9 %fusion.7 = (bf16[1,64,16,64]{3,0,2,1:T(2,128)(2,1)S(1)}, bf16[1,64,16,64]{3,0,2,1:T(2,128)(2,1)S(1)}) fusion(s32[]{:T(128)S(6)} %select_n.95, bf16[4,64,16,64]{3,0,2,1:T(4,128)(2,1)S(1)} %bitcast.57, s32[]{:T(128)S(6)} %select_n.94), kind=kLoop, calls=%fused_computation.32 | loop fusion | flops 524288 | bytes 786440 | tf_op jit(solution)/shard_map/concatenate | solution.py:38
  41.4 3.0 collective-permute-start.3
  45.7 7.6 %collective-permute-done = bf16[1,64,16,64]{3,0,2,1:T(2,128)(2,1)S(1)} collective-permute-done((bf16[1,64,16,64]{3,0,2,1:T(2,128)(2,1)S(1)}, bf16[1,64,16,64]{3,0,2,1:T(2,128)(2,1)S(1)}, u32[]{:S(2)}, u32[]{:S(2)}) %collective-permute-start) | collective-permute-done | bytes 131104 | tf_op jit(solution)/shard_map/ppermute | solution.py:44
  53.3 2.5 collective-permute-start.5
  55.8 8.3 %collective-permute-done.1 = bf16[1,64,16,64]{3,0,2,1:T(2,128)(2,1)} collective-permute-done((bf16[1,64,16,64]{3,0,2,1:T(2,128)(2,1)}, bf16[1,64,16,64]{3,0,2,1:T(2,128)(2,1)}, u32[]{:S(2)}, u32[]{:S(2)}) %collective-permute-start.1) | collective-permute-done | bytes 131104 | tf_op jit(solution)/shard_map/ppermute | solution.py:44
  64.1 2.7 collective-permute-start.6
  67.9 7.5 %collective-permute-done.2 = bf16[1,64,16,64]{3,0,2,1:T(2,128)(2,1)S(1)} collective-permute-done((bf16[1,64,16,64]{3,0,2,1:T(2,128)(2,1)}, bf16[1,64,16,64]{3,0,2,1:T(2,128)(2,1)S(1)}, u32[]{:S(2)}, u32[]{:S(2)}) %collective-permute-start.2) | collective-permute-done | bytes 131104 | tf_op jit(solution)/shard_map/ppermute | solution.py:44
  75.6 39.3 %collective-permute-done.4 = bf16[1,64,16,64]{3,0,2,1:T(2,128)(2,1)S(1)} collective-permute-done((bf16[1,64,16,64]{3,0,2,1:T(2,128)(2,1)}, bf16[1,64,16,64]{3,0,2,1:T(2,128)(2,1)S(1)}, u32[]{:S(2)}, u32[]{:S(2)}) %collective-permute-start.4) | collective-permute-done | bytes 131104 | tf_op jit(solution)/shard_map/ppermute | solution.py:44
  115.1 2.2 gather_fusion
  118.2 6.4 %copy.99 = bf16[64,128,256]{1,2,0:T(8,128)(2,1)} copy(bf16[64,128,256]{2,1,0:T(8,128)(2,1)} %param.8) | data formatting | bytes 8388608 | tf_op args[2]
  124.6 4.6 constant_dynamic-slice_fusion.1
  129.4 22.0 %collective-permute-start.8 = (bf16[64,128,64]{1,2,0:T(8,128)(2,1)}, bf16[64,128,64]{1,2,0:T(8,128)(2,1)}, u32[]{:S(2)}, u32[]{:S(2)}) collective-permute-start(bf16[64,128,64]{1,2,0:T(8,128)(2,1)} %get-tuple-element.11), channel_id=1, source_target_pairs={{0,8},{4,12},{8,0},{12,4},{16,24},{20,28},{24,16},{28,20},{1,9},{5... | collective-permute-start | bytes 3145736 | tf_op jit(solution)/shard_map/ppermute | solution.py:60
  151.4 2.2 collective-permute-start.9
  156.4 18.8 %collective-permute-done.7 = bf16[64,128,64]{1,2,0:T(8,128)(2,1)} collective-permute-done((bf16[64,128,64]{1,2,0:T(8,128)(2,1)}, bf16[64,128,64]{1,2,0:T(8,128)(2,1)}, u32[]{:S(2)}, u32[]{:S(2)}) %collective-permute-start.7) | collective-permute-done | bytes 1048608 | tf_op jit(solution)/shard_map/ppermute | solution.py:60
  177.3 2.5 concatenate.23
  179.8 2.0 copy.102
  181.8 2.5 concatenate.24
  184.4 10.2 %collective-permute-done.9 = bf16[64,128,64]{1,2,0:T(8,128)(2,1)} collective-permute-done((bf16[64,128,64]{1,2,0:T(8,128)(2,1)}, bf16[64,128,64]{1,2,0:T(8,128)(2,1)}, u32[]{:S(2)}, u32[]{:S(2)}) %collective-permute-start.9) | collective-permute-done | bytes 1048608 | tf_op jit(solution)/shard_map/ppermute | solution.py:60
  196.6 2.5 concatenate.25
  199.1 3.6 pad_maximum_fusion
  202.7 9.3 %copy.96 = bf16[64,8,4,16,64]{4,3,2,1,0:T(8,128)(2,1)} copy(bf16[64,8,4,16,64]{4,3,0,1,2:T(8,128)(2,1)} %bitcast.58) | data formatting | bytes 8388608 | tf_op jit(solution)/shard_map/transpose | solution.py:48
  212.0 35.1 %all-gather.4.cloned.1.call-done = bf16[16,512,128]{2,1,0:T(8,128)(2,1)} async-done(((bf16[16,64,128]{2,1,0:T(8,128)(2,1)}), bf16[16,512,128]{2,1,0:T(8,128)(2,1)}) %all-gather.4.cloned.1.call-update) | async-done | bytes 2097168 | tf_op jit(solution)/shard_map/all_gather | solution.py:34
  247.1 16.1 %convert_bitcast_fusion = bf16[16,64,128,64]{2,3,0,1:T(8,128)(2,1)} fusion(bf16[64,512,64,1]{2,1,3,0:T(8,128)(2,1)} %bitcast.54, bf16[16,512,128]{2,1,0:T(8,128)(2,1)} %all-gather.4.cloned.1.call-done), kind=kOutput, calls=%fused_computation.3 | convolution fusion | flops 8598323200 | bytes 23068672 | tf_op jit(solution)/shard_map/acq,pcd->padq/dot_general | solution.py:62
  263.2 30.3 %copy.98 = bf16[16,64,128,64]{3,2,1,0:T(8,128)(2,1)} copy(bf16[16,64,128,64]{2,3,0,1:T(8,128)(2,1)} %convert_bitcast_fusion) | data formatting | bytes 33554432 | tf_op jit(solution)/shard_map/convert_element_type | solution.py:64
  293.5 44.0 %reshape.110 = bf16[16,64,8192,1]{2,1,0,3:T(8,128)(2,1)} reshape(bf16[16,64,128,64]{3,2,1,0:T(8,128)(2,1)} %copy.98) | data formatting | bytes 33554432 | tf_op jit(solution)/shard_map/dot_general | solution.py:66
  337.6 12.2 %fusion = f32[16,64,4,64]{3,1,2,0:T(8,128)S(1)} fusion(bf16[4,64,8192,1]{2,1,0,3:T(8,128)(2,1)} %bitcast.59, bf16[16,64,8192,1]{2,1,0,3:T(8,128)(2,1)} %reshape.110), kind=kOutput, calls=%fused_computation.1 | convolution fusion | flops 4294967296 | bytes 22020096 | tf_op jit(solution)/shard_map/dot_general | solution.py:66
  350.3 2.7 copy.104
  353.0 2.5 reshape.96
  357.4 30.0 %reduce-scatter.3.cloned.1.call-done = f32[16,64,128]{2,1,0:T(8,128)} async-done(((f32[16,64,512]{2,1,0:T(8,128)}), f32[16,64,128]{2,1,0:T(8,128)}) %reduce-scatter.3.cloned.1.call-update) | async-done | bytes 524304 | tf_op jit(solution)/shard_map/reduce_scatter | solution.py:80
  388.1 64.9 %reduce-scatter.5.cloned.1.call-done = f32[2,64,128]{2,1,0:T(8,128)} async-done(((f32[16,64,128]{2,1,0:T(8,128)}), f32[2,64,128]{2,1,0:T(8,128)}) %reduce-scatter.5.cloned.1.call-update) | async-done | bytes 65552 | tf_op jit(solution)/shard_map/reduce_scatter | solution.py:81
  (62 shorter events, 18.6 us)
Async XLA Ops:
  6.5 1.6 copy-start
  6.5 196.2 %all-gather.6.cloned.1.call-start = ((), (), s32[]{:S(2)}) async-start(), calls=%async_computation.5 | async-start | bytes 10485760 | tf_op jit(solution)/shard_map/all_gather | solution.py:47
  31.9 32.2 %collective-permute-start.1 = (bf16[1,64,16,64]{3,0,2,1:T(2,128)(2,1)}, bf16[1,64,16,64]{3,0,2,1:T(2,128)(2,1)}, u32[]{:S(2)}, u32[]{:S(2)}) collective-permute-start(bf16[1,64,16,64]{3,0,2,1:T(2,128)(2,1)} %get-tuple-element.14), channel_id=1, source_target_pairs={{0,8},{4,12},{8,0},{12,4},{16,24},{20,28},{24,16},{28,20},{1,9},{5... | collective-permute-start | bytes 393224 | tf_op jit(solution)/shard_map/ppermute | solution.py:44
  39.8 13.4 %collective-permute-start = (bf16[1,64,16,64]{3,0,2,1:T(2,128)(2,1)S(1)}, bf16[1,64,16,64]{3,0,2,1:T(2,128)(2,1)S(1)}, u32[]{:S(2)}, u32[]{:S(2)}) collective-permute-start(bf16[1,64,16,64]{3,0,2,1:T(2,128)(2,1)S(1)} %get-tuple-element.19), channel_id=1, source_target_pairs={{0,4},{4,0},{8,12},{12,8},{16,20},{20,16},{24,28},{28,24},{1,5},{5... | collective-permute-start | bytes 393224 | tf_op jit(solution)/shard_map/ppermute | solution.py:44
  41.4 34.1 %collective-permute-start.2 = (bf16[1,64,16,64]{3,0,2,1:T(2,128)(2,1)}, bf16[1,64,16,64]{3,0,2,1:T(2,128)(2,1)S(1)}, u32[]{:S(2)}, u32[]{:S(2)}) collective-permute-start(bf16[1,64,16,64]{3,0,2,1:T(2,128)(2,1)} %get-tuple-element.15), channel_id=1, source_target_pairs={{0,12},{4,8},{8,4},{12,0},{16,28},{20,24},{24,20},{28,16},{1,13},{... | collective-permute-start | bytes 393224 | tf_op jit(solution)/shard_map/ppermute | solution.py:44
  41.4 34.1 %collective-permute-start.3 = (bf16[1,64,16,64]{3,0,2,1:T(2,128)(2,1)}, bf16[1,64,16,64]{3,0,2,1:T(2,128)(2,1)S(1)}, u32[]{:S(2)}, u32[]{:S(2)}) collective-permute-start(bf16[1,64,16,64]{3,0,2,1:T(2,128)(2,1)} %get-tuple-element.16), channel_id=1, source_target_pairs={{0,16},{4,20},{8,24},{12,28},{16,0},{20,4},{24,8},{28,12},{1,17},{... | collective-permute-start | bytes 393224 | tf_op jit(solution)/shard_map/ppermute | solution.py:44
  44.4 70.5 %collective-permute-start.4 = (bf16[1,64,16,64]{3,0,2,1:T(2,128)(2,1)}, bf16[1,64,16,64]{3,0,2,1:T(2,128)(2,1)S(1)}, u32[]{:S(2)}, u32[]{:S(2)}) collective-permute-start(bf16[1,64,16,64]{3,0,2,1:T(2,128)(2,1)} %get-tuple-element.17), channel_id=1, source_target_pairs={{0,20},{4,16},{8,28},{12,24},{16,4},{20,0},{24,12},{28,8},{1,21},{... | collective-permute-start | bytes 393224 | tf_op jit(solution)/shard_map/ppermute | solution.py:44
  53.3 61.7 %collective-permute-start.5 = (bf16[1,64,16,64]{3,0,2,1:T(2,128)(2,1)S(1)}, bf16[1,64,16,64]{3,0,2,1:T(2,128)(2,1)S(1)}, u32[]{:S(2)}, u32[]{:S(2)}) collective-permute-start(bf16[1,64,16,64]{3,0,2,1:T(2,128)(2,1)S(1)} %get-tuple-element.18), channel_id=1, source_target_pairs={{0,24},{4,28},{8,16},{12,20},{16,8},{20,12},{24,0},{28,4},{1,25},{... | collective-permute-start | bytes 393224 | tf_op jit(solution)/shard_map/ppermute | solution.py:44
  64.1 50.9 %collective-permute-start.6 = (bf16[1,64,16,64]{3,0,2,1:T(2,128)(2,1)S(1)}, bf16[1,64,16,64]{3,0,2,1:T(2,128)(2,1)S(1)}, u32[]{:S(2)}, u32[]{:S(2)}) collective-permute-start(bf16[1,64,16,64]{3,0,2,1:T(2,128)(2,1)S(1)} %get-tuple-element.13), channel_id=1, source_target_pairs={{0,28},{4,24},{8,20},{12,16},{16,12},{20,8},{24,4},{28,0},{1,29},{... | collective-permute-start | bytes 393224 | tf_op jit(solution)/shard_map/ppermute | solution.py:44
  117.3 129.8 %all-gather.4.cloned.1.call-start = ((), (), s32[]{:S(2)}) async-start(), calls=%async_computation.2 | async-start | bytes 2359296 | tf_op jit(solution)/shard_map/all_gather | solution.py:34
  118.0 269.4 %reduce-scatter.3.cloned.1.call-start = ((), (), s32[]{:S(2)}) async-start(), calls=%async_computation.3 | async-start | bytes 2621440 | tf_op jit(solution)/shard_map/reduce_scatter | solution.py:80
  129.1 46.1 %collective-permute-start.7 = (bf16[64,128,64]{1,2,0:T(8,128)(2,1)}, bf16[64,128,64]{1,2,0:T(8,128)(2,1)}, u32[]{:S(2)}, u32[]{:S(2)}) collective-permute-start(bf16[64,128,64]{1,2,0:T(8,128)(2,1)} %get-tuple-element.12), channel_id=1, source_target_pairs={{0,4},{4,8},{8,12},{12,0},{16,20},{20,24},{24,28},{28,16},{1,5},{5... | collective-permute-start | bytes 3145736 | tf_op jit(solution)/shard_map/ppermute | solution.py:60
  129.4 50.5 %collective-permute-start.8 = (bf16[64,128,64]{1,2,0:T(8,128)(2,1)}, bf16[64,128,64]{1,2,0:T(8,128)(2,1)}, u32[]{:S(2)}, u32[]{:S(2)}) collective-permute-start(bf16[64,128,64]{1,2,0:T(8,128)(2,1)} %get-tuple-element.11), channel_id=1, source_target_pairs={{0,8},{4,12},{8,0},{12,4},{16,24},{20,28},{24,16},{28,20},{1,9},{5... | collective-permute-start | bytes 3145736 | tf_op jit(solution)/shard_map/ppermute | solution.py:60
  151.4 43.1 %collective-permute-start.9 = (bf16[64,128,64]{1,2,0:T(8,128)(2,1)}, bf16[64,128,64]{1,2,0:T(8,128)(2,1)}, u32[]{:S(2)}, u32[]{:S(2)}) collective-permute-start(bf16[64,128,64]{1,2,0:T(8,128)(2,1)} %get-tuple-element.10), channel_id=1, source_target_pairs={{0,12},{4,0},{8,4},{12,8},{16,28},{20,16},{24,20},{28,24},{1,13},{... | collective-permute-start | bytes 3145736 | tf_op jit(solution)/shard_map/ppermute | solution.py:60
  355.6 99.0 %copy-start.1 = (bf16[64,64,256]{2,1,0:T(8,128)(2,1)S(1)}, bf16[64,64,256]{2,1,0:T(8,128)(2,1)}, u32[]{:S(2)}) copy-start(bf16[64,64,256]{2,1,0:T(8,128)(2,1)} %param.7) | copy-start | bytes 6291460
  357.3 30.2 %copy-start.4 = (f32[512]{0:T(512)S(1)}, f32[512]{0:T(512)}, u32[]{:S(2)}) copy-start(f32[512]{0:T(512)} %param.11) | copy-start | bytes 6148
  357.3 30.2 %copy-start.2 = (s32[2,2]{1,0:T(2,128)S(1)}, s32[2,2]{1,0:T(2,128)}, u32[]{:S(2)}) copy-start(s32[2,2]{1,0:T(2,128)} %param.9) | copy-start | bytes 52
  357.3 30.4 %copy-start.3 = (f32[128]{0:T(128)S(1)}, f32[128]{0:T(128)}, u32[]{:S(2)}) copy-start(f32[128]{0:T(128)} %param.10) | copy-start | bytes 1540
  357.3 30.7 %slice-start = ((f32[512]{0:T(512)}), f32[64]{0:T(128)S(1)}, s32[]{:S(2)}) async-start(f32[512]{0:T(512)} %param.11), calls=%async_computation.6 | async-start | bytes 1024 | tf_op jit(solution)/shard_map/slice | solution.py:91
  357.4 95.6 %reduce-scatter.5.cloned.1.call-start = ((), (), s32[]{:S(2)}) async-start(), calls=%async_computation.4 | async-start | bytes 589824 | tf_op jit(solution)/shard_map/reduce_scatter | solution.py:81
Sparse Core Ops, SparseCore 0:
  117.4 78.0 all-gather.5
  197.7 49.4 all-gather.3
  357.5 29.9 reduce-scatter.2
  391.0 61.9 reduce-scatter.4
